TPU v7x, 32 devices: a whole 2x2x4 slice. The times are simulated.
32 devices in a mesh: req: 16 (over z, x, core), ep: 2 (over y).
Axes of the slice: x: 2, y: 2, z: 4, core: 2. Of those that a mesh axis runs over, the one named last changes fastest.
Arguments:
- hidden: bfloat16 [16, 512, 1536], P('req', None, 'ep'), may hold values from -6 to 6
- key_cache: bfloat16 [16, 8, 2560, 64], P('req', 'ep'), may hold values from -160 to 160
- value_cache: bfloat16 [16, 8, 2560, 64], P('req', 'ep'), may hold values from -6 to 6
- request_order: int32 [16], replicated, may hold values from 0 to 15, each once
- cached_lengths: int32 [16], replicated, may hold values from 1 to 2048, 16384 in all
- expert_ids: int32 [16, 512, 8], P('req'), may hold values from 0 to 39, all different within a row; in each aligned block of 512 rows (0 to 511, 512 to 1023, ..., all dimensions but the last counted through in order) at most 192 rows name the same one
- gate_values: float32 [16, 512, 8], P('req'), may hold values from 0.1 to 1
- attn_gain: float32 [1536], replicated, may hold values from 0.25 to 1.75
- ffn_gain: float32 [1536], replicated, may hold values from 0.25 to 1.75
- w_query: bfloat16 [1536, 1536], P(None, 'ep'), may hold values from -0.15625 to 0.15625
- w_key: bfloat16 [1536, 512], P(None, 'ep'), may hold values from -0.15625 to 0.15625
- w_value: bfloat16 [1536, 512], P(None, 'ep'), may hold values from -0.15625 to 0.15625
- w_out: bfloat16 [1536, 1536], P('ep'), may hold values from -0.15625 to 0.15625
- expert_gate: bfloat16 [4, 1536, 512], P('ep', 'req'), may hold values from -0.15625 to 0.15625
- expert_up: bfloat16 [4, 1536, 512], P('ep', 'req'), may hold values from -0.15625 to 0.15625
- expert_down: bfloat16 [4, 512, 1536], P('ep', 'req'), may hold values from -0.25 to 0.25
Outputs:
- hidden_out: bfloat16 [16, 512, 1536], P('req', None, 'ep')
- key_cache_out: bfloat16 [16, 8, 2560, 64], P('req', 'ep')
- value_cache_out: bfloat16 [16, 8, 2560, 64], P('req', 'ep')
Inputs may be any that keep to these rules, and one draw needn't show every extreme that they name: Slot s holds request request_order[s]; every request is held by one slot. `cached_lengths`: the longest cached length is exactly 2048. `expert_ids`: each token names 8 different experts; among the 512 tokens of one slot no expert is named by more than 192 tokens, a bound that some block reaches.
All inputs are finite; a program needn't handle non-finite values.
Results may differ from a plain program's by a relative error of at most 0.012.
The roundings to bfloat16 on the way count: a program that leaves them out, or rounds other values in their place, can miss the bound.
Values may be sent and summed in bfloat16 or wider, within the bound.
No kernel may reach another device: no remote copies, remote signals or barrier semaphores. Data moves between devices by JAX's collectives and lax.ppermute only.
A program may use at most 128 MiB of HBM per device.

v0:
```python
import jax
import jax.numpy as jnp
from jax import lax
from jax.sharding import PartitionSpec as P

epsilon = 1e-06


def normalize(values, gain):
    return values * lax.rsqrt(jnp.mean(values * values, -1, keepdims=True) + epsilon) * gain


def rotate(values, positions):
    half = values.shape[-1] // 2
    freq = 10000.0 ** (-jnp.arange(half, dtype=jnp.float32) * (2.0 / values.shape[-1]))
    angle = positions.astype(jnp.float32)[:, None] * freq[None, :]
    cosine = jnp.cos(angle)
    sine = jnp.sin(angle)
    first = values[..., :half]
    second = values[..., half:]
    return jnp.concatenate([first * cosine - second * sine, second * cosine + first * sine], -1)


def rounded(values):
    return lax.optimization_barrier(values.astype(jnp.bfloat16)).astype(jnp.float32)


def route_tables(chosen, gate_rows, wanted, capacity):
    hits = chosen[:, :, None] == wanted[None, None, :]
    member = jnp.sum(hits.astype(jnp.int32), 1, dtype=jnp.int32)
    weight = jnp.sum(jnp.where(hits, gate_rows[:, :, None], 0.0), 1)
    place = jnp.cumsum(member, 0, dtype=jnp.int32) - 1
    slots = jnp.arange(capacity, dtype=jnp.int32)
    table = (member.T[:, None, :] == 1) & (place.T[:, None, :] == slots[None, :, None])
    gate_slot = jnp.sum(jnp.where(table, weight.T[:, None, :], 0.0), 2)
    return (table.astype(jnp.bfloat16), gate_slot)


def attend(query, keys, values, length, new_rows):
    query_rows = query.shape[1]
    blocks = keys.shape[1] // new_rows
    limit = length + jnp.arange(query_rows, dtype=jnp.int32) % new_rows
    scale = query.shape[2] ** (-0.5)

    def visit(carry, block):
        running, total, summed = carry
        start = block * new_rows
        key_block = lax.dynamic_slice_in_dim(keys, start, new_rows, 1)
        value_block = lax.dynamic_slice_in_dim(values, start, new_rows, 1)
        scores = (
            jnp.einsum("kqd,kjd->kqj", query, key_block, preferred_element_type=jnp.float32) * scale
        )
        column = start + jnp.arange(new_rows, dtype=jnp.int32)
        visible = column[None, :] <= limit[:, None]
        scores = jnp.where(visible[None], scores, -1e30)
        highest = jnp.maximum(running, jnp.max(scores, -1))
        correction = jnp.exp(running - highest)
        probs = jnp.where(visible[None], jnp.exp(scores - highest[..., None]), 0.0)
        total = total * correction + jnp.sum(probs, -1)
        summed = summed * correction[..., None] + jnp.einsum(
            "kqj,kjd->kqd",
            probs.astype(jnp.bfloat16),
            value_block,
            preferred_element_type=jnp.float32,
        )
        return ((highest, total, summed), None)

    start_state = (
        jnp.full(query.shape[:2], -1e30, jnp.float32),
        jnp.zeros(query.shape[:2], jnp.float32),
        jnp.zeros(query.shape, jnp.float32),
    )
    final, unused = lax.scan(visit, start_state, jnp.arange(blocks, dtype=jnp.int32))
    return final[2] / final[1][..., None]


def on_device(
    hidden,
    key_cache,
    value_cache,
    request_order,
    cached_lengths,
    expert_ids,
    gate_values,
    attn_gain,
    ffn_gain,
    w_query,
    w_key,
    w_value,
    w_out,
    expert_gate,
    expert_up,
    expert_down,
):
    own_rows = hidden[0]
    new_rows = own_rows.shape[0]
    own_width = own_rows.shape[1]
    head_dim = key_cache.shape[3]
    kv_local = key_cache.shape[1]
    heads_local = w_query.shape[1] // head_dim
    group = heads_local // kv_local
    per_device = expert_gate.shape[0]
    devices = lax.axis_size("ep")
    capacity = 3 * new_rows // 8
    everyone = jnp.arange(request_order.shape[0], dtype=jnp.int32)
    request = jnp.sum(jnp.where(everyone == lax.axis_index("req"), request_order, 0))
    length = jnp.sum(jnp.where(everyone == request, cached_lengths, 0))
    rows_whole = lax.all_gather(own_rows, "ep", axis=1, tiled=True)
    width = rows_whole.shape[1]
    normed = normalize(rows_whole.astype(jnp.float32), attn_gain).astype(jnp.bfloat16)
    query = jnp.dot(normed, w_query, preferred_element_type=jnp.float32)
    key_new = jnp.dot(normed, w_key, preferred_element_type=jnp.float32)
    value_new = jnp.dot(normed, w_value, preferred_element_type=jnp.float32)
    positions = length + jnp.arange(new_rows, dtype=jnp.int32)
    query = rotate(
        query.reshape(new_rows, heads_local, head_dim).transpose(1, 0, 2), positions
    ).astype(jnp.bfloat16)
    query = query.reshape(kv_local, group * new_rows, head_dim)
    key_new = rotate(
        key_new.reshape(new_rows, kv_local, head_dim).transpose(1, 0, 2), positions
    ).astype(jnp.bfloat16)
    value_new = (
        value_new.reshape(new_rows, kv_local, head_dim).transpose(1, 0, 2).astype(jnp.bfloat16)
    )
    zero = jnp.zeros((), jnp.int32)
    keys = lax.dynamic_update_slice(key_cache[0], key_new, (zero, length, zero))
    values = lax.dynamic_update_slice(value_cache[0], value_new, (zero, length, zero))
    attended = attend(query, keys, values, length, new_rows)
    attended = (
        attended.reshape(heads_local, new_rows, head_dim)
        .transpose(1, 0, 2)
        .reshape(new_rows, heads_local * head_dim)
        .astype(jnp.bfloat16)
    )
    partial_value = rounded(jnp.dot(attended, w_out, preferred_element_type=jnp.float32))
    head_sum = lax.psum_scatter(
        partial_value.astype(jnp.bfloat16), "ep", scatter_dimension=1, tiled=True
    ).astype(jnp.float32)
    mixed = (own_rows.astype(jnp.float32) + head_sum).astype(jnp.bfloat16)
    mixed_f = mixed.astype(jnp.float32)
    chosen = expert_ids[0]
    gate_rows = gate_values[0]
    first = lax.axis_index("ep") * per_device
    squares = jnp.sum(mixed_f * mixed_f, -1)
    totals = lax.psum(squares, "ep")
    local_gain = lax.dynamic_slice_in_dim(ffn_gain, lax.axis_index("ep") * own_width, own_width)
    normed_cols = (mixed_f * lax.rsqrt(totals / width + epsilon)[:, None] * local_gain).astype(
        jnp.bfloat16
    )
    table_all, gate_all = route_tables(
        chosen, gate_rows, jnp.arange(per_device * devices, dtype=jnp.int32), capacity
    )
    buffers = jnp.einsum(
        "ect,td->ecd", table_all, normed_cols, preferred_element_type=jnp.float32
    ).astype(jnp.bfloat16)
    inputs = lax.all_to_all(buffers, "ep", split_axis=0, concat_axis=2, tiled=True)
    gate_own = lax.dynamic_slice_in_dim(gate_all, first, per_device, 0)
    columns = inputs
    gate_next = jnp.einsum(
        "ecd,edf->ecf",
        columns,
        lax.all_gather(expert_gate, "req", axis=1, tiled=True),
        preferred_element_type=jnp.float32,
    )
    up_next = jnp.einsum(
        "ecd,edf->ecf",
        columns,
        lax.all_gather(expert_up, "req", axis=1, tiled=True),
        preferred_element_type=jnp.float32,
    )
    hidden_act = (jax.nn.silu(gate_next) * up_next).astype(jnp.bfloat16)
    columns = hidden_act
    output = jnp.einsum(
        "ecf,efd->ecd",
        columns,
        lax.all_gather(expert_down, "req", axis=1, tiled=True),
        preferred_element_type=jnp.float32,
    )
    contrib = (output * gate_own[..., None]).astype(jnp.bfloat16)
    returned = lax.all_to_all(contrib, "ep", split_axis=2, concat_axis=0, tiled=True)
    per_expert = jnp.einsum("ect,ecd->etd", table_all, returned, preferred_element_type=jnp.float32)
    grouped = rounded(jnp.sum(per_expert.reshape(devices, per_device, new_rows, own_width), 1))
    expert_sum = jnp.sum(grouped, 0)
    result = (mixed_f + expert_sum).astype(jnp.bfloat16)
    return (result[None], keys[None], values[None])


def solution(mesh):
    in_specs = (
        P("req", None, "ep"),
        P("req", "ep", None, None),
        P("req", "ep", None, None),
        P(),
        P(),
        P("req", None, None),
        P("req", None, None),
        P(),
        P(),
        P(None, "ep"),
        P(None, "ep"),
        P(None, "ep"),
        P("ep", None),
        P("ep", "req", None),
        P("ep", "req", None),
        P("ep", "req", None),
    )
    out_specs = (P("req", None, "ep"), P("req", "ep", None, None), P("req", "ep", None, None))
    return jax.shard_map(
        on_device, mesh=mesh, in_specs=in_specs, out_specs=out_specs, check_vma=False
    )
```

profile of v0, /device:TPU:16, one launch (start us, length us, event | category | flops | bytes accessed | tf_op | source)
XLA Modules:
  0.0 387.9 jit_solution(1194642636352865639)
XLA Ops:
  8.1 2.6 copy.81
  10.7 1.1 copy.82
  12.5 1.3 fusion.60
  16.7 23.5 %all-gather.12.cloned.1.call-done = bf16[1,512,1536]{2,1,0:T(8,128)(2,1)} async-done(((bf16[1,512,768]{2,1,0:T(8,128)(2,1)}), bf16[1,512,1536]{2,1,0:T(8,128)(2,1)}) %all-gather.12.cloned.1.call-update) | async-done | bytes 1572880 | tf_op jit(solution)/shard_map/all_gather | solution.py:108
  40.2 1.9 fusion.24
  42.2 2.1 fusion.66
  44.3 1.6 fusion.64
  45.9 1.0 subtract_convert_fusion
  47.1 1.1 concatenate.14
  48.2 1.2 copy.52
  49.4 1.1 concatenate.15
  50.5 1.6 pad_maximum_fusion
  52.1 1.0 copy.53
  53.2 4.0 %dynamic_update_slice.6 = bf16[4,2560,64]{1,2,0:T(8,128)(2,1)} dynamic-update-slice(bf16[4,2560,64]{1,2,0:T(8,128)(2,1)} %bitcast.102, bf16[4,512,64]{1,2,0:T(8,128)(2,1)S(1)} %pad_maximum_fusion.1, s32[]{:T(128)} %constant.31.clone.1, s32[]{:T(128)S(6)} %select_n.46, s32[]{:T(128)} %constant.31.clone.1) | dynamic-update-slice | bytes 524292 | tf_op jit(solution)/shard_map/dynamic_update_slice | solution.py:126
  57.1 2.4 convolution_convert_fusion.1
  59.5 3.8 dynamic_update_slice.7
  63.3 123.9 %while.15 = (s32[]{:T(128)}, f32[4,1536]{1,0:T(4,128)S(1)}, f32[4,1536]{1,0:T(4,128)S(1)}, f32[4,1536,64]{1,2,0:T(8,128)}, s32[5]{0:T(128)S(1)}, /*index=5*/bf16...) while((s32[]{:T(128)}, f32[4,1536]{1,0:T(4,128)S(1)}, ...), condition=%wide.region_6.7_spmd.clone, body=%wide.region_3.6_spmd.clone.sunk | while | flops 848208896 | bytes 96092400 | solution.py:73
  63.3 0.7 dynamic_slice.33
  65.9 8.1 %fusion.93 = (f32[4,1536]{1,0:T(4,128)S(1)}, f32[4,512,1536]{2,1,0:T(8,128)}) fusion(pred[1536,512]{0,1:T(8,128)(4,1)S(1)} %broadcast_compare_fusion.3, bf16[4,1536,64]{1,2,0:T(8,128)(2,1)} %get-tuple-element.236, bf16[4,2560,64]{1,2,0:T(8,128)(2,1)} %get-tuple-element.235, s32[]{:T(128)S(6)} %select_n.102), kind=kOutput, calls=%fused_computation.3.clone.1 | convolution fusion | flops 412084224 | bytes 14442500 | tf_op jit(solution)/shard_map/while/body/eval_jaxpr/kqd,kjd->kqj/dot_general | solution.py:51
  73.9 6.9 %fusion.94 = f32[4,1536]{1,0:T(4,128)S(1)} fusion(f32[4,512,1536]{2,1,0:T(8,128)} %get-tuple-element.201, f32[4,1536]{1,0:T(4,128)S(1)} %select_maximum_fusion.2, pred[1536,512]{0,1:T(8,128)(4,1)S(1)} %broadcast_compare_fusion.3), kind=kLoop, calls=%fused_computation.5.clone.1 | loop fusion | flops 15722496 | bytes 13418496 | tf_op jit(solution)/shard_map/while/body/eval_jaxpr/reduce_sum | solution.py:59
  80.8 1.4 copy-done.1
  82.2 5.7 %fusion.96 = f32[4,1536,64]{1,2,0:T(8,128)} fusion(f32[4,512,1536]{2,1,0:T(8,128)S(1)} %copy-done.1, f32[4,1536]{1,0:T(4,128)S(1)} %select_maximum_fusion.2, pred[1536,512]{0,1:T(8,128)(4,1)S(1)} %broadcast_compare_fusion.3, f32[4,1536,64]{1,2,0:T(8,128)} %get-tuple-element.220, f32[4,1536]{1,0:T(4,128)S(1)} %get-tuple-element.203, pred[]{:T(512)S(6)} %compare.4, ...), kind=kOutput, calls=%fused_computation.8.clone.1 | convolution fusion | flops 419561472 | bytes 16826372 | tf_op jit(solution)/shard_map/while/body/eval_jaxpr/kqj,kjd->kqd/dot_general | solution.py:60
  87.9 0.7 dynamic_slice.33
  90.4 8.1 %fusion.93 = (f32[4,1536]{1,0:T(4,128)S(1)}, f32[4,512,1536]{2,1,0:T(8,128)}) fusion(pred[1536,512]{0,1:T(8,128)(4,1)S(1)} %broadcast_compare_fusion.3, bf16[4,1536,64]{1,2,0:T(8,128)(2,1)} %get-tuple-element.236, bf16[4,2560,64]{1,2,0:T(8,128)(2,1)} %get-tuple-element.235, s32[]{:T(128)S(6)} %select_n.102), kind=kOutput, calls=%fused_computation.3.clone.1 | convolution fusion | flops 412084224 | bytes 14442500 | tf_op jit(solution)/shard_map/while/body/eval_jaxpr/kqd,kjd->kqj/dot_general | solution.py:51
  98.5 6.9 %fusion.94 = f32[4,1536]{1,0:T(4,128)S(1)} fusion(f32[4,512,1536]{2,1,0:T(8,128)} %get-tuple-element.201, f32[4,1536]{1,0:T(4,128)S(1)} %select_maximum_fusion.2, pred[1536,512]{0,1:T(8,128)(4,1)S(1)} %broadcast_compare_fusion.3), kind=kLoop, calls=%fused_computation.5.clone.1 | loop fusion | flops 15722496 | bytes 13418496 | tf_op jit(solution)/shard_map/while/body/eval_jaxpr/reduce_sum | solution.py:59
  105.4 1.4 copy-done.1
  106.8 6.0 %fusion.96 = f32[4,1536,64]{1,2,0:T(8,128)} fusion(f32[4,512,1536]{2,1,0:T(8,128)S(1)} %copy-done.1, f32[4,1536]{1,0:T(4,128)S(1)} %select_maximum_fusion.2, pred[1536,512]{0,1:T(8,128)(4,1)S(1)} %broadcast_compare_fusion.3, f32[4,1536,64]{1,2,0:T(8,128)} %get-tuple-element.220, f32[4,1536]{1,0:T(4,128)S(1)} %get-tuple-element.203, pred[]{:T(512)S(6)} %compare.4, ...), kind=kOutput, calls=%fused_computation.8.clone.1 | convolution fusion | flops 419561472 | bytes 16826372 | tf_op jit(solution)/shard_map/while/body/eval_jaxpr/kqj,kjd->kqd/dot_general | solution.py:60
  112.7 0.7 dynamic_slice.33
  115.3 8.1 %fusion.93 = (f32[4,1536]{1,0:T(4,128)S(1)}, f32[4,512,1536]{2,1,0:T(8,128)}) fusion(pred[1536,512]{0,1:T(8,128)(4,1)S(1)} %broadcast_compare_fusion.3, bf16[4,1536,64]{1,2,0:T(8,128)(2,1)} %get-tuple-element.236, bf16[4,2560,64]{1,2,0:T(8,128)(2,1)} %get-tuple-element.235, s32[]{:T(128)S(6)} %select_n.102), kind=kOutput, calls=%fused_computation.3.clone.1 | convolution fusion | flops 412084224 | bytes 14442500 | tf_op jit(solution)/shard_map/while/body/eval_jaxpr/kqd,kjd->kqj/dot_general | solution.py:51
  123.4 6.9 %fusion.94 = f32[4,1536]{1,0:T(4,128)S(1)} fusion(f32[4,512,1536]{2,1,0:T(8,128)} %get-tuple-element.201, f32[4,1536]{1,0:T(4,128)S(1)} %select_maximum_fusion.2, pred[1536,512]{0,1:T(8,128)(4,1)S(1)} %broadcast_compare_fusion.3), kind=kLoop, calls=%fused_computation.5.clone.1 | loop fusion | flops 15722496 | bytes 13418496 | tf_op jit(solution)/shard_map/while/body/eval_jaxpr/reduce_sum | solution.py:59
  130.3 1.4 copy-done.1
  131.6 6.0 %fusion.96 = f32[4,1536,64]{1,2,0:T(8,128)} fusion(f32[4,512,1536]{2,1,0:T(8,128)S(1)} %copy-done.1, f32[4,1536]{1,0:T(4,128)S(1)} %select_maximum_fusion.2, pred[1536,512]{0,1:T(8,128)(4,1)S(1)} %broadcast_compare_fusion.3, f32[4,1536,64]{1,2,0:T(8,128)} %get-tuple-element.220, f32[4,1536]{1,0:T(4,128)S(1)} %get-tuple-element.203, pred[]{:T(512)S(6)} %compare.4, ...), kind=kOutput, calls=%fused_computation.8.clone.1 | convolution fusion | flops 419561472 | bytes 16826372 | tf_op jit(solution)/shard_map/while/body/eval_jaxpr/kqj,kjd->kqd/dot_general | solution.py:60
  137.6 0.7 dynamic_slice.33
  140.1 8.1 %fusion.93 = (f32[4,1536]{1,0:T(4,128)S(1)}, f32[4,512,1536]{2,1,0:T(8,128)}) fusion(pred[1536,512]{0,1:T(8,128)(4,1)S(1)} %broadcast_compare_fusion.3, bf16[4,1536,64]{1,2,0:T(8,128)(2,1)} %get-tuple-element.236, bf16[4,2560,64]{1,2,0:T(8,128)(2,1)} %get-tuple-element.235, s32[]{:T(128)S(6)} %select_n.102), kind=kOutput, calls=%fused_computation.3.clone.1 | convolution fusion | flops 412084224 | bytes 14442500 | tf_op jit(solution)/shard_map/while/body/eval_jaxpr/kqd,kjd->kqj/dot_general | solution.py:51
  148.2 6.9 %fusion.94 = f32[4,1536]{1,0:T(4,128)S(1)} fusion(f32[4,512,1536]{2,1,0:T(8,128)} %get-tuple-element.201, f32[4,1536]{1,0:T(4,128)S(1)} %select_maximum_fusion.2, pred[1536,512]{0,1:T(8,128)(4,1)S(1)} %broadcast_compare_fusion.3), kind=kLoop, calls=%fused_computation.5.clone.1 | loop fusion | flops 15722496 | bytes 13418496 | tf_op jit(solution)/shard_map/while/body/eval_jaxpr/reduce_sum | solution.py:59
  155.1 1.4 copy-done.1
  156.5 6.0 %fusion.96 = f32[4,1536,64]{1,2,0:T(8,128)} fusion(f32[4,512,1536]{2,1,0:T(8,128)S(1)} %copy-done.1, f32[4,1536]{1,0:T(4,128)S(1)} %select_maximum_fusion.2, pred[1536,512]{0,1:T(8,128)(4,1)S(1)} %broadcast_compare_fusion.3, f32[4,1536,64]{1,2,0:T(8,128)} %get-tuple-element.220, f32[4,1536]{1,0:T(4,128)S(1)} %get-tuple-element.203, pred[]{:T(512)S(6)} %compare.4, ...), kind=kOutput, calls=%fused_computation.8.clone.1 | convolution fusion | flops 419561472 | bytes 16826372 | tf_op jit(solution)/shard_map/while/body/eval_jaxpr/kqj,kjd->kqd/dot_general | solution.py:60
  162.4 0.7 dynamic_slice.33
  165.0 8.1 %fusion.93 = (f32[4,1536]{1,0:T(4,128)S(1)}, f32[4,512,1536]{2,1,0:T(8,128)}) fusion(pred[1536,512]{0,1:T(8,128)(4,1)S(1)} %broadcast_compare_fusion.3, bf16[4,1536,64]{1,2,0:T(8,128)(2,1)} %get-tuple-element.236, bf16[4,2560,64]{1,2,0:T(8,128)(2,1)} %get-tuple-element.235, s32[]{:T(128)S(6)} %select_n.102), kind=kOutput, calls=%fused_computation.3.clone.1 | convolution fusion | flops 412084224 | bytes 14442500 | tf_op jit(solution)/shard_map/while/body/eval_jaxpr/kqd,kjd->kqj/dot_general | solution.py:51
  173.0 6.9 %fusion.94 = f32[4,1536]{1,0:T(4,128)S(1)} fusion(f32[4,512,1536]{2,1,0:T(8,128)} %get-tuple-element.201, f32[4,1536]{1,0:T(4,128)S(1)} %select_maximum_fusion.2, pred[1536,512]{0,1:T(8,128)(4,1)S(1)} %broadcast_compare_fusion.3), kind=kLoop, calls=%fused_computation.5.clone.1 | loop fusion | flops 15722496 | bytes 13418496 | tf_op jit(solution)/shard_map/while/body/eval_jaxpr/reduce_sum | solution.py:59
  179.9 1.4 copy-done.1
  181.3 6.0 %fusion.96 = f32[4,1536,64]{1,2,0:T(8,128)} fusion(f32[4,512,1536]{2,1,0:T(8,128)S(1)} %copy-done.1, f32[4,1536]{1,0:T(4,128)S(1)} %select_maximum_fusion.2, pred[1536,512]{0,1:T(8,128)(4,1)S(1)} %broadcast_compare_fusion.3, f32[4,1536,64]{1,2,0:T(8,128)} %get-tuple-element.220, f32[4,1536]{1,0:T(4,128)S(1)} %get-tuple-element.203, pred[]{:T(512)S(6)} %compare.4, ...), kind=kOutput, calls=%fused_computation.8.clone.1 | convolution fusion | flops 419561472 | bytes 16826372 | tf_op jit(solution)/shard_map/while/body/eval_jaxpr/kqj,kjd->kqd/dot_general | solution.py:60
  187.3 1.5 divide_convert_fusion
  188.8 1.5 copy.54
  190.3 1.8 convert_element_type.91
  192.6 2.6 convolution_convert_fusion
  197.0 1.2 reduce-window.6
  198.8 22.6 %reduce-scatter.2.cloned.1.call-done = bf16[512,768]{1,0:T(8,128)(2,1)} async-done(((bf16[512,1536]{1,0:T(8,128)(2,1)}), bf16[512,768]{1,0:T(8,128)(2,1)}) %reduce-scatter.2.cloned.1.call-update) | async-done | bytes 786448 | tf_op jit(solution)/shard_map/reduce_scatter | solution.py:136
  221.4 1.5 fusion.28
  222.9 5.2 %psum.7 = f32[512]{0:T(512)S(1)} all-reduce(f32[512]{0:T(512)S(1)} %fusion.28), channel_id=1, replica_groups=mesh['req'=16,'ep'=2] {'ep'}, use_global_device_ids=true, to_apply=%region_12.13 | all-reduce | flops 512 | bytes 4096 | tf_op jit(solution)/shard_map/psum | solution.py:145
  228.1 3.2 fusion.40
  231.3 4.6 %all-to-all-start = ((bf16[4,192,768]{2,1,0:T(8,128)(2,1)}), bf16[4,192,768]{2,1,0:T(8,128)(2,1)}, u32[]{:S(2)}, u32[]{:S(2)}) async-start(bf16[4,192,768]{2,1,0:T(8,128)(2,1)} %fusion.40), calls=%async_computation.1 | async-start | bytes 2359296 | tf_op jit(solution)/shard_map/all_to_all | solution.py:156
  236.3 14.2 %all-to-all-done = bf16[4,192,768]{2,1,0:T(8,128)(2,1)} async-done(((bf16[4,192,768]{2,1,0:T(8,128)(2,1)}), bf16[4,192,768]{2,1,0:T(8,128)(2,1)}, u32[]{:S(2)}, u32[]{:S(2)}) %all-to-all-start) | async-done | bytes 1179680 | tf_op jit(solution)/shard_map/all_to_all | solution.py:156
  250.5 2.4 copy.61
  252.9 3.9 %fusion.68 = f32[2,192,512]{2,1,0:T(8,128)} fusion(bf16[2,192,1536]{2,1,0:T(8,128)(2,1)} %bitcast.104, bf16[2,1536,512]{2,1,0:T(8,128)(2,1)} %all-gather.6.cloned.1.call-done), kind=kOutput, calls=%fused_computation.100 | convolution fusion | flops 603979776 | bytes 5111808 | tf_op jit(solution)/shard_map/ecd,edf->ecf/dot_general | solution.py:159
  256.8 31.7 %all-gather.10.cloned.1.call-done = bf16[2,512,1536]{2,1,0:T(8,128)(2,1)} async-done(((bf16[2,32,1536]{2,1,0:T(8,128)(2,1)}), bf16[2,512,1536]{2,1,0:T(8,128)(2,1)}) %all-gather.10.cloned.1.call-update) | async-done | bytes 3145744 | tf_op jit(solution)/shard_map/all_gather | solution.py:176
  288.5 46.1 %all-gather.8.cloned.1.call-done = bf16[2,1536,512]{2,1,0:T(8,128)(2,1)} async-done(((bf16[2,96,512]{2,1,0:T(8,128)(2,1)}), bf16[2,1536,512]{2,1,0:T(8,128)(2,1)}) %all-gather.8.cloned.1.call-update) | async-done | bytes 3145744 | tf_op jit(solution)/shard_map/all_gather | solution.py:168
  334.7 5.9 %fusion.27 = bf16[2,192,1536]{2,1,0:T(8,128)(2,1)} fusion(bf16[2,512,1536]{2,1,0:T(8,128)(2,1)} %all-gather.10.cloned.1.call-done, f32[2,192]{1,0:T(2,128)S(1)} %constant_dynamic-slice_fusion, bf16[2,192,1536]{2,1,0:T(8,128)(2,1)} %bitcast.105, bf16[2,1536,512]{2,1,0:T(8,128)(2,1)} %all-gather.8.cloned.1.call-done, f32[2,192,512]{2,1,0:T(8,128)} %fusion.68), kind=kOutput, calls=%fused_computation.39 | convolution fusion | flops 1210318848 | bytes 9438720 | tf_op jit(solution)/shard_map/ecf,efd->ecd/dot_general | solution.py:173
  340.6 4.8 %copy.57 = bf16[2,192,1536]{1,0,2:T(2,128)(2,1)} copy(bf16[2,192,1536]{2,1,0:T(8,128)(2,1)} %fusion.27) | data formatting | bytes 2359296 | tf_op jit(solution)/shard_map/convert_element_type | solution.py:179
  345.4 25.2 %all_to_all.36 = bf16[2,192,1536]{1,0,2:T(2,128)(2,1)} all-to-all(bf16[2,192,1536]{1,0,2:T(2,128)(2,1)} %copy.57), channel_id=1, replica_groups=mesh['req'=16,'ep'=2] {'ep'}, dimensions={2} | all-to-all | bytes 2359296 | tf_op jit(solution)/shard_map/all_to_all | solution.py:180
  370.6 4.9 %copy.58 = bf16[2,192,2,768]{3,1,0,2:T(8,128)(2,1)} copy(bf16[2,192,2,768]{1,0,3,2:T(2,128)(2,1)} %bitcast.101) | data formatting | bytes 2359296 | tf_op jit(solution)/shard_map/all_to_all | solution.py:180
  375.5 2.5 bitcast_reduce_fusion
  378.3 0.9 copy-done.3
  379.1 1.2 fusion.44
  (95 shorter events, 11.6 us)
Async XLA Ops:
  8.0 184.6 %copy-start = (bf16[768,1536]{1,0:T(8,128)(2,1)S(1)}, bf16[768,1536]{1,0:T(8,128)(2,1)}, u32[]{:S(2)}) copy-start(bf16[768,1536]{1,0:T(8,128)(2,1)} %param.30) | copy-start | bytes 7077892
  8.0 32.2 %all-gather.12.cloned.1.call-start = ((), (), s32[]{:S(2)}) async-start(), calls=%async_computation.7 | async-start | bytes 2359296 | tf_op jit(solution)/shard_map/all_gather | solution.py:108
  8.1 2.6 copy-start.5
  10.7 1.2 copy-start.11
  10.7 1.8 copy-start.12
  11.8 30.4 %copy-start.10 = (f32[1536]{0:T(1024)S(1)}, f32[1536]{0:T(1024)}, u32[]{:S(2)}) copy-start(f32[1536]{0:T(1024)} %param.25) | copy-start | bytes 18436
  11.8 209.7 %reduce-scatter.2.cloned.1.call-start = ((), (), s32[]{:S(2)}) async-start(), calls=%async_computation.3 | async-start | bytes 2359296 | tf_op jit(solution)/shard_map/reduce_scatter | solution.py:136
  40.2 1.9 copy-start.4
  42.2 2.2 copy-start.9
  73.9 8.3 %copy-start.1 = (f32[4,512,1536]{2,1,0:T(8,128)S(1)}, f32[4,512,1536]{2,1,0:T(8,128)}, u32[]{:S(2)}) copy-start(f32[4,512,1536]{2,1,0:T(8,128)} %get-tuple-element.201) | copy-start | bytes 37748740 | tf_op jit(solution)/shard_map/while
  98.5 8.3 %copy-start.1 = (f32[4,512,1536]{2,1,0:T(8,128)S(1)}, f32[4,512,1536]{2,1,0:T(8,128)}, u32[]{:S(2)}) copy-start(f32[4,512,1536]{2,1,0:T(8,128)} %get-tuple-element.201) | copy-start | bytes 37748740 | tf_op jit(solution)/shard_map/while
  123.3 8.3 %copy-start.1 = (f32[4,512,1536]{2,1,0:T(8,128)S(1)}, f32[4,512,1536]{2,1,0:T(8,128)}, u32[]{:S(2)}) copy-start(f32[4,512,1536]{2,1,0:T(8,128)} %get-tuple-element.201) | copy-start | bytes 37748740 | tf_op jit(solution)/shard_map/while
  148.2 8.3 %copy-start.1 = (f32[4,512,1536]{2,1,0:T(8,128)S(1)}, f32[4,512,1536]{2,1,0:T(8,128)}, u32[]{:S(2)}) copy-start(f32[4,512,1536]{2,1,0:T(8,128)} %get-tuple-element.201) | copy-start | bytes 37748740 | tf_op jit(solution)/shard_map/while
  173.0 8.3 %copy-start.1 = (f32[4,512,1536]{2,1,0:T(8,128)S(1)}, f32[4,512,1536]{2,1,0:T(8,128)}, u32[]{:S(2)}) copy-start(f32[4,512,1536]{2,1,0:T(8,128)} %get-tuple-element.201) | copy-start | bytes 37748740 | tf_op jit(solution)/shard_map/while
  195.2 1.8 copy-start.6
  195.2 3.5 copy-start.8
  195.2 26.3 %copy-start.2 = (bf16[1,512,768]{2,1,0:T(8,128)(2,1)S(1)}, bf16[1,512,768]{2,1,0:T(8,128)(2,1)}, u32[]{:S(2)}) copy-start(bf16[1,512,768]{2,1,0:T(8,128)(2,1)} %param.18) | copy-start | bytes 2359300
  195.2 57.7 %all-gather.6.cloned.1.call-start = ((), (), s32[]{:S(2)}) async-start(), calls=%async_computation.4 | async-start | bytes 3342336 | tf_op jit(solution)/shard_map/all_gather | solution.py:162
  195.8 92.8 %all-gather.10.cloned.1.call-start = ((), (), s32[]{:S(2)}) async-start(), calls=%async_computation.6 | async-start | bytes 3342336 | tf_op jit(solution)/shard_map/all_gather | solution.py:176
  196.4 138.3 %all-gather.8.cloned.1.call-start = ((), (), s32[]{:S(2)}) async-start(), calls=%async_computation.5 | async-start | bytes 3342336 | tf_op jit(solution)/shard_map/all_gather | solution.py:168
  231.3 4.6 %copy-start.7 = (f32[1,512,8]{1,2,0:T(8,128)S(1)}, f32[1,512,8]{1,2,0:T(8,128)}, u32[]{:S(2)}) copy-start(f32[1,512,8]{1,2,0:T(8,128)} %param.24) | copy-start | bytes 49156
  231.3 19.2 %all-to-all-start = ((bf16[4,192,768]{2,1,0:T(8,128)(2,1)}), bf16[4,192,768]{2,1,0:T(8,128)(2,1)}, u32[]{:S(2)}, u32[]{:S(2)}) async-start(bf16[4,192,768]{2,1,0:T(8,128)(2,1)} %fusion.40), calls=%async_computation.1 | async-start | bytes 2359296 | tf_op jit(solution)/shard_map/all_to_all | solution.py:156
  378.0 1.1 copy-start.3
Sparse Core Ops, SparseCore 0:
  11.9 28.2 all-gather.11
  195.3 26.0 reduce-scatter.1
Sparse Core Ops, SparseCore 1:
  198.0 44.6 all-gather.5
  244.8 43.7 all-gather.9
  291.0 43.7 all-gather.7
where the time goes:
time: 392 us; the launch traced here: 388 us
  waiting for transfers between devices  140 us (36%)
  matrix products  93.9 us (24%)
  other arithmetic  54.2 us (14%)
  local copies, waits for them, and re-layouts  43.3 us (11%)
  blocking collectives  30.4 us (8%)
  between operations  17.8 us (5%)
  starting transfers between devices  4.8 us (1%)
    all_gather x1, waiting for transfers between devices, on_device(): lax.all_gather(expert_up, 'req', axis=1, tiled=True)  46.1 us
    dot_general x5, matrix products, visit(): jnp.einsum('kqd,kjd->kqj', query, key_block, preferred_element_type=jnp.f...  40.3 us
    reduce_sum x5, other arithmetic, visit(): total = total * correction + jnp.sum(probs, -1)  34.3 us
    all_gather x1, waiting for transfers between devices, on_device(): lax.all_gather(expert_down, 'req', axis=1, tiled=True)  31.7 us
    dot_general x5, matrix products, visit(): jnp.einsum('kqj,kjd->kqd', probs.astype(jnp.bfloat16), value_block, prefe...  29.5 us
    all_to_all x1, blocking collectives, on_device(): lax.all_to_all(contrib, 'ep', split_axis=2, concat_axis=0, tiled=True)  25.2 us
    all_gather x1, waiting for transfers between devices, on_device(): rows_whole = lax.all_gather(own_rows, 'ep', axis=1, tiled=True)  23.5 us
    reduce_scatter x1, waiting for transfers between devices, on_device(): lax.psum_scatter(partial_value.astype(jnp.bfloat16), 'ep', scatter_dimens...  22.6 us
  transfers between devices with their start and end apart: 6, of which 5 were waited for; matrix products, arithmetic and copies ran while one was open for 4% of the time, Pallas kernels for 0%

commit v1 on v0

v1 whole, which is shorter than its diff:
```python
import jax
import jax.numpy as jnp
from jax import lax
from jax.experimental import pallas as pl
from jax.experimental.pallas import tpu as pltpu
from jax.sharding import PartitionSpec as P

epsilon = 1e-06


def normalize(values, gain):
    return values * lax.rsqrt(jnp.mean(values * values, -1, keepdims=True) + epsilon) * gain


def rotate(values, positions):
    half = values.shape[-1] // 2
    freq = 10000.0 ** (-jnp.arange(half, dtype=jnp.float32) * (2.0 / values.shape[-1]))
    angle = positions.astype(jnp.float32)[:, None] * freq[None, :]
    cosine = jnp.cos(angle)
    sine = jnp.sin(angle)
    first = values[..., :half]
    second = values[..., half:]
    return jnp.concatenate([first * cosine - second * sine, second * cosine + first * sine], -1)


def rounded(values):
    return lax.optimization_barrier(values.astype(jnp.bfloat16)).astype(jnp.float32)


def route_tables(chosen, gate_rows, wanted, capacity):
    hits = chosen[:, :, None] == wanted[None, None, :]
    member = jnp.sum(hits.astype(jnp.int32), 1, dtype=jnp.int32)
    weight = jnp.sum(jnp.where(hits, gate_rows[:, :, None], 0.0), 1)
    place = jnp.cumsum(member, 0, dtype=jnp.int32) - 1
    slots = jnp.arange(capacity, dtype=jnp.int32)
    table = (member.T[:, None, :] == 1) & (place.T[:, None, :] == slots[None, :, None])
    gate_slot = jnp.sum(jnp.where(table, weight.T[:, None, :], 0.0), 2)
    return (table.astype(jnp.bfloat16), gate_slot)


def flash_attend(query, keys, values, length, new_rows):
    kv_heads, rows, head_dim = query.shape
    block = new_rows
    blocks = keys.shape[1] // block
    scale = head_dim ** (-0.5)
    limit = (length + jnp.arange(rows, dtype=jnp.int32) % new_rows)[:, None]

    def last_block(length_ref):
        return (length_ref[0] + new_rows - 1) // block

    def kernel(length_ref, limit_ref, q_ref, k_ref, v_ref, o_ref, m_sc, l_sc, acc_sc):
        step = pl.program_id(1)

        @pl.when(step == 0)
        def _():
            m_sc[...] = jnp.full(m_sc.shape, -1e30, jnp.float32)
            l_sc[...] = jnp.zeros(l_sc.shape, jnp.float32)
            acc_sc[...] = jnp.zeros(acc_sc.shape, jnp.float32)

        def visit(masked):
            scores = (
                lax.dot_general(
                    q_ref[0],
                    k_ref[0],
                    (((1,), (1,)), ((), ())),
                    preferred_element_type=jnp.float32,
                )
                * scale
            )
            if masked:
                column = step * block + lax.broadcasted_iota(jnp.int32, scores.shape, 1)
                visible = column <= limit_ref[...]
                scores = jnp.where(visible, scores, -1e30)
            previous = m_sc[...]
            highest = jnp.maximum(previous, jnp.max(scores, -1, keepdims=True))
            probs = jnp.exp(scores - highest)
            if masked:
                probs = jnp.where(visible, probs, 0.0)
            correction = jnp.exp(previous - highest)
            l_sc[...] = l_sc[...] * correction + jnp.sum(probs, -1, keepdims=True)
            acc_sc[...] = acc_sc[...] * correction + jnp.dot(
                probs.astype(jnp.bfloat16), v_ref[0], preferred_element_type=jnp.float32
            )
            m_sc[...] = highest

        whole = (step + 1) * block - 1 <= length_ref[0]

        @pl.when(whole)
        def _():
            visit(False)

        @pl.when(jnp.logical_not(whole) & (step <= last_block(length_ref)))
        def _():
            visit(True)

        @pl.when(step == blocks - 1)
        def _():
            o_ref[0] = (acc_sc[...] / l_sc[...]).astype(o_ref.dtype)

    def kv_map(head, step, length_ref):
        return (head, jnp.minimum(step, last_block(length_ref)), 0)

    grid_spec = pltpu.PrefetchScalarGridSpec(
        num_scalar_prefetch=1,
        grid=(kv_heads, blocks),
        in_specs=[
            pl.BlockSpec((rows, 1), lambda head, step, length_ref: (0, 0)),
            pl.BlockSpec((1, rows, head_dim), lambda head, step, length_ref: (head, 0, 0)),
            pl.BlockSpec((1, block, head_dim), kv_map),
            pl.BlockSpec((1, block, head_dim), kv_map),
        ],
        out_specs=pl.BlockSpec((1, rows, head_dim), lambda head, step, length_ref: (head, 0, 0)),
        scratch_shapes=[
            pltpu.VMEM((rows, 1), jnp.float32),
            pltpu.VMEM((rows, 1), jnp.float32),
            pltpu.VMEM((rows, head_dim), jnp.float32),
        ],
    )
    flops = 4 * kv_heads * rows * keys.shape[1] * head_dim
    return pl.pallas_call(
        kernel,
        grid_spec=grid_spec,
        out_shape=jax.ShapeDtypeStruct(query.shape, jnp.bfloat16),
        compiler_params=pltpu.CompilerParams(dimension_semantics=("arbitrary", "arbitrary")),
        cost_estimate=pl.CostEstimate(
            flops=flops,
            transcendentals=kv_heads * rows * keys.shape[1],
            bytes_accessed=2 * (query.size + keys.size + values.size + query.size),
        ),
    )(length.reshape(1), limit, query, keys, values)


def shifted(values, shift):
    devices = lax.axis_size("ep")
    return lax.ppermute(values, "ep", [(i, (i + shift) % devices) for i in range(devices)])


def gather_columns(values):
    devices = lax.axis_size("ep")
    me = lax.axis_index("ep")
    width = values.shape[-1]
    whole = jnp.zeros(values.shape[:-1] + (width * devices,), values.dtype)
    for shift in range(devices):
        piece = values if shift == 0 else shifted(values, shift)
        source = (me - shift) % devices
        whole = lax.dynamic_update_slice_in_dim(whole, piece, source * width, values.ndim - 1)
    return whole


def sum_over_ep(part):
    devices = lax.axis_size("ep")
    total = part.astype(jnp.float32)
    for shift in range(1, devices):
        total = total + shifted(part, shift).astype(jnp.float32)
    return total


def scatter_sum_over_ep(part, width):
    devices = lax.axis_size("ep")
    me = lax.axis_index("ep")
    total = lax.dynamic_slice_in_dim(part, me * width, width, 1).astype(jnp.float32)
    for shift in range(1, devices):
        target = (me + shift) % devices
        piece = lax.dynamic_slice_in_dim(part, target * width, width, 1)
        total = total + shifted(piece, shift).astype(jnp.float32)
    return total


def on_device(
    hidden,
    key_cache,
    value_cache,
    request_order,
    cached_lengths,
    expert_ids,
    gate_values,
    attn_gain,
    ffn_gain,
    w_query,
    w_key,
    w_value,
    w_out,
    expert_gate,
    expert_up,
    expert_down,
):
    own_rows = hidden[0]
    new_rows = own_rows.shape[0]
    own_width = own_rows.shape[1]
    head_dim = key_cache.shape[3]
    kv_local = key_cache.shape[1]
    heads_local = w_query.shape[1] // head_dim
    group = heads_local // kv_local
    per_device = expert_gate.shape[0]
    capacity = 3 * new_rows // 8
    me = lax.axis_index("ep")
    gate_whole = lax.all_gather(expert_gate, "req", axis=1, tiled=True)
    up_whole = lax.all_gather(expert_up, "req", axis=1, tiled=True)
    down_whole = lax.all_gather(expert_down, "req", axis=1, tiled=True)
    everyone = jnp.arange(request_order.shape[0], dtype=jnp.int32)
    request = jnp.sum(jnp.where(everyone == lax.axis_index("req"), request_order, 0))
    length = jnp.sum(jnp.where(everyone == request, cached_lengths, 0))
    rows_whole = gather_columns(own_rows)
    rows_f = rows_whole.astype(jnp.float32)
    normed = normalize(rows_f, attn_gain).astype(jnp.bfloat16)
    query = jnp.dot(normed, w_query, preferred_element_type=jnp.float32)
    key_new = jnp.dot(normed, w_key, preferred_element_type=jnp.float32)
    value_new = jnp.dot(normed, w_value, preferred_element_type=jnp.float32)
    positions = length + jnp.arange(new_rows, dtype=jnp.int32)
    query = rotate(
        query.reshape(new_rows, heads_local, head_dim).transpose(1, 0, 2), positions
    ).astype(jnp.bfloat16)
    query = query.reshape(kv_local, group * new_rows, head_dim)
    key_new = rotate(
        key_new.reshape(new_rows, kv_local, head_dim).transpose(1, 0, 2), positions
    ).astype(jnp.bfloat16)
    value_new = (
        value_new.reshape(new_rows, kv_local, head_dim).transpose(1, 0, 2).astype(jnp.bfloat16)
    )
    zero = jnp.zeros((), jnp.int32)
    keys = lax.dynamic_update_slice(key_cache[0], key_new, (zero, length, zero))
    values = lax.dynamic_update_slice(value_cache[0], value_new, (zero, length, zero))
    attended = flash_attend(query, keys, values, length, new_rows)
    gate_whole, up_whole, down_whole, attended = lax.optimization_barrier(
        (gate_whole, up_whole, down_whole, attended)
    )
    attended = (
        attended.reshape(heads_local, new_rows, head_dim)
        .transpose(1, 0, 2)
        .reshape(new_rows, heads_local * head_dim)
    )
    head_part = jnp.dot(attended, w_out, preferred_element_type=jnp.float32).astype(jnp.bfloat16)
    head_sum = sum_over_ep(head_part)
    mixed_f = (rows_f + head_sum).astype(jnp.bfloat16).astype(jnp.float32)
    ffn_normed = normalize(mixed_f, ffn_gain).astype(jnp.bfloat16)
    table, gate_slot = route_tables(
        expert_ids[0],
        gate_values[0],
        me * per_device + jnp.arange(per_device, dtype=jnp.int32),
        capacity,
    )
    dispatched = jnp.einsum(
        "ect,td->ecd", table, ffn_normed, preferred_element_type=jnp.float32
    ).astype(jnp.bfloat16)
    gate_act = jnp.einsum("ecd,edf->ecf", dispatched, gate_whole, preferred_element_type=jnp.float32)
    up_act = jnp.einsum("ecd,edf->ecf", dispatched, up_whole, preferred_element_type=jnp.float32)
    act = (jax.nn.silu(gate_act) * up_act).astype(jnp.bfloat16)
    output = jnp.einsum("ecf,efd->ecd", act, down_whole, preferred_element_type=jnp.float32)
    contrib = (output * gate_slot[..., None]).astype(jnp.bfloat16)
    expert_part = jnp.einsum(
        "ect,ecd->td", table, contrib, preferred_element_type=jnp.float32
    ).astype(jnp.bfloat16)
    expert_sum = scatter_sum_over_ep(expert_part, own_width)
    mixed_own = lax.dynamic_slice_in_dim(mixed_f, me * own_width, own_width, 1)
    result = (mixed_own + expert_sum).astype(jnp.bfloat16)
    return (result[None], keys[None], values[None])


def solution(mesh):
    in_specs = (
        P("req", None, "ep"),
        P("req", "ep", None, None),
        P("req", "ep", None, None),
        P(),
        P(),
        P("req", None, None),
        P("req", None, None),
        P(),
        P(),
        P(None, "ep"),
        P(None, "ep"),
        P(None, "ep"),
        P("ep", None),
        P("ep", "req", None),
        P("ep", "req", None),
        P("ep", "req", None),
    )
    out_specs = (P("req", None, "ep"), P("req", "ep", None, None), P("req", "ep", None, None))
    return jax.shard_map(
        on_device, mesh=mesh, in_specs=in_specs, out_specs=out_specs, check_vma=False
    )
```

time: 392 us -> 237 us (0.60)
  waiting for transfers between devices: 140 us -> 51.5 us
  Pallas kernels: 0 us -> 79.9 us
  matrix products: 93.9 us -> 18 us
  other arithmetic: 54.2 us -> 20.5 us
  blocking collectives: 30.4 us -> 0 us
    all_gather x4 -> x3, waiting for transfers between devices: 101 us -> 5.47 us  [the longest x1 5.47 us: on_device(): down_whole = lax.all_gather(expert_down, 'req', axis=1, tiled=True)]
    pallas_call x0 -> x1, Pallas kernels: none -> 79.9 us  [flash_attend(): pl.pallas_call(kernel, grid_spec=grid_spec, out_shape=jax.ShapeDtypeStruc...]
    dot_general x14 -> x4, matrix products: 85.3 us -> 7.15 us  [the longest x1 4.63 us: on_device(): jnp.einsum('ect,ecd->td', table, contrib, preferred_element_type=jnp.floa...]
    ppermute x0 -> x3, waiting for transfers between devices: none -> 43.9 us  [shifted(): lax.ppermute(values, 'ep', [(i, (i + shift) % devices) for i in range(dev...]
    reduce_sum x7 -> x0, other arithmetic: 36 us -> none  [the longest x5 34.3 us: visit(): total = total * correction + jnp.sum(probs, -1)]
    all_to_all x1 -> x0, blocking collectives: 25.2 us -> none  [on_device(): lax.all_to_all(contrib, 'ep', split_axis=2, concat_axis=0, tiled=True)]
    reduce_scatter x1 -> x0, waiting for transfers between devices: 22.6 us -> none  [on_device(): lax.psum_scatter(partial_value.astype(jnp.bfloat16), 'ep', scatter_dimens...]
    all_to_all x1 -> x0, waiting for transfers between devices: 14.2 us -> none  [on_device(): lax.all_to_all(buffers, 'ep', split_axis=0, concat_axis=2, tiled=True)]
  transfers between devices with their start and end apart: 6 -> 6, of which waited for: 5 -> 4; matrix products, arithmetic and copies ran while one was open for 4% -> 26% of each run, Pallas kernels for 0% -> 34%
where the time goes in v1:
time: 237 us; the launch traced here: 234 us
  Pallas kernels  79.9 us (34%)
  waiting for transfers between devices  51.5 us (22%)
  local copies, waits for them, and re-layouts  43.1 us (18%)
  other arithmetic  20.5 us (9%)
  matrix products  18 us (8%)
  between operations  15.9 us (7%)
  starting transfers between devices  4.72 us (2%)
    pallas_call x1, Pallas kernels, flash_attend(): pl.pallas_call(kernel, grid_spec=grid_spec, out_shape=jax.ShapeDtypeStruc...  79.9 us
    ppermute x3, waiting for transfers between devices, shifted(): lax.ppermute(values, 'ep', [(i, (i + shift) % devices) for i in range(dev...  43.9 us
    unnamed x29, local copies, waits for them, and re-layouts  18.9 us
    all_gather x1, waiting for transfers between devices, on_device(): down_whole = lax.all_gather(expert_down, 'req', axis=1, tiled=True)  5.47 us
    dynamic_update_slice x1, local copies, waits for them, and re-layouts, on_device(): keys = lax.dynamic_update_slice(key_cache[0], key_new, (zero, length, zero))  4.96 us
    dynamic_update_slice x1, local copies, waits for them, and re-layouts, on_device(): lax.dynamic_update_slice(value_cache[0], value_new, (zero, length, zero))  4.94 us
    another operation x2, local copies, waits for them, and re-layouts  4.77 us
  transfers between devices with their start and end apart: 6, of which 4 were waited for; matrix products, arithmetic and copies ran while one was open for 26% of the time, Pallas kernels for 34%

profile of v1, /device:TPU:16, one launch (start us, length us, event | category | flops | bytes accessed | tf_op | source)
XLA Modules:
  0.0 233.6 jit_solution(17360647506225663795)
XLA Ops:
  7.2 0.0 copy-start
  7.2 0.0 all-gather.4.cloned.1.call-start
  7.2 0.7 all-gather.4.cloned.1.call-update
  7.9 0.0 all-gather.6.cloned.1.call-start
  8.0 0.7 all-gather.6.cloned.1.call-update
  8.7 0.0 all-gather.8.cloned.1.call-start
  8.7 0.7 all-gather.8.cloned.1.call-update
  9.4 1.6 collective-permute-start
  11.0 1.3 fusion.26
  12.3 2.0 fusion.27
  14.2 0.6 add_convert_fusion.3
  15.5 0.3 multiply_cosine_fusion
  15.8 0.8 copy.57
  16.7 0.8 copy.58
  18.1 3.9 %copy.55 = bf16[1,4,2560,64]{3,2,1,0:T(8,128)(2,1)} copy(bf16[1,4,2560,64]{2,3,1,0:T(8,128)(2,1)} %param.17) | data formatting | bytes 2621440 | tf_op args[1]
  22.0 3.9 %copy.59 = bf16[1,4,2560,64]{3,2,1,0:T(8,128)(2,1)} copy(bf16[1,4,2560,64]{2,3,1,0:T(8,128)(2,1)} %param.18) | data formatting | bytes 2621440 | tf_op args[2]
  26.5 1.6 fusion.12.limit_ref
  28.1 0.1 broadcast_in_dim.35
  28.2 0.0 copy-start.10
  28.2 0.1 constant_dynamic-update-slice_fusion.1
  28.3 0.8 collective-permute-done
  29.1 1.2 constant_dynamic-update-slice_fusion
  30.3 0.4 fusion
  30.7 1.6 fusion.29
  32.3 1.4 copy.56
  33.6 3.1 %convolution_convert_fusion.2 = bf16[512,256]{0,1:T(8,128)(2,1)} fusion(bf16[1536,256]{1,0:T(8,128)(2,1)} %param.27, bf16[512,1536]{1,0:T(8,128)(2,1)} %copy-done.2, f32[1536]{0:T(1024)S(1)} %copy-done.11, f32[512]{0:T(512)S(1)} %add_rsqrt_fusion.1), kind=kOutput, calls=%fused_computation.23 | convolution fusion | flops 405929984 | bytes 2629632 | tf_op jit(solution)/shard_map/dot_general | solution.py:208
  36.7 2.0 copy.60
  38.7 3.7 %fusion.31 = f32[512,768]{0,1:T(8,128)S(1)} fusion(bf16[1536,768]{1,0:T(8,128)(2,1)} %param.25, bf16[512,1536]{1,0:T(8,128)(2,1)} %copy-done.2, f32[1536]{0:T(1024)S(1)} %copy-done.11, f32[512]{0:T(512)S(1)} %add_rsqrt_fusion.1), kind=kOutput, calls=%fused_computation.66 | convolution fusion | flops 1211105280 | bytes 5513216 | tf_op jit(solution)/shard_map/dot_general | solution.py:206
  42.4 1.1 subtract_convert_fusion.1
  43.5 2.4 %copy.53 = bf16[12,512,32]{2,1,0:T(8,128)(2,1)} copy(bf16[12,512,32]{1,2,0:T(8,128)(2,1)} %get-tuple-element.25) | data formatting | bytes 786432 | tf_op jit(solution)/shard_map/convert.5
  45.9 2.4 %copy.54 = bf16[12,512,32]{2,1,0:T(8,128)(2,1)} copy(bf16[12,512,32]{1,2,0:T(8,128)(2,1)} %get-tuple-element.26) | data formatting | bytes 786432 | tf_op jit(solution)/shard_map/convert.4
  48.3 1.5 subtract_convert_fusion
  49.8 0.3 pad_maximum_fusion.1
  50.1 5.0 %dynamic_update_slice.14.k_ref = bf16[4,2560,64]{2,1,0:T(8,128)(2,1)} dynamic-update-slice(bf16[4,2560,64]{2,1,0:T(8,128)(2,1)} %bitcast.53, bf16[4,512,64]{2,1,0:T(8,128)(2,1)S(1)} %pad_maximum_fusion.1, s32[]{:T(128)} %constant.60.clone.1, s32[]{:T(128)S(6)} %select_n.67, s32[]{:T(128)} %constant.60.clone.1) | dynamic-update-slice | bytes 524292 | tf_op jit(solution)/shard_map/dynamic_update_slice | solution.py:221
  55.0 4.9 %dynamic_update_slice.15.v_ref = bf16[4,2560,64]{2,1,0:T(8,128)(2,1)} dynamic-update-slice(bf16[4,2560,64]{2,1,0:T(8,128)(2,1)} %bitcast.51, bf16[4,512,64]{2,1,0:T(8,128)(2,1)S(1)} %bitcast.59, s32[]{:T(128)} %constant.60.clone.1, s32[]{:T(128)S(6)} %select_n.67, s32[]{:T(128)} %constant.60.clone.1) | dynamic-update-slice | bytes 524292 | tf_op jit(solution)/shard_map/dynamic_update_slice | solution.py:222
  60.0 3.9 %pad_maximum_fusion.q_ref = bf16[4,1536,64]{2,1,0:T(8,128)(2,1)} fusion(bf16[4,1536,32]{2,1,0:T(8,128)(2,1)} %bitcast.57, bf16[4,1536,32]{2,1,0:T(8,128)(2,1)} %bitcast.56), kind=kLoop, calls=%fused_computation.17 | loop fusion | flops 1572864 | bytes 1572864 | tf_op jit(solution)/shard_map/concatenate | solution.py:23
  63.9 79.9 %shard_map.175 = bf16[4,1536,64]{2,1,0:T(8,128)(2,1)} custom-call(s32[1]{0:T(128)} %bitcast.1.length_ref, s32[1536,1]{1,0:T(8,128)} %fusion.12.limit_ref, bf16[4,1536,64]{2,1,0:T(8,128)(2,1)} %pad_maximum_fusion.q_ref, bf16[4,2560,64]{2,1,0:T(8,128)(2,1)} %dynamic_update_slice.14.k_ref, bf16[4,2560,64]{2,1,0:T(8,128)(2,1)} %dynamic_update_slice.15.v_ref), custom_call_target="tpu_custom_call" | custom-call | flops 4026531840 | bytes 4194304 | tf_op jit(solution)/shard_map/pallas_call | solution.py:120
  143.8 5.5 %all-gather.8.cloned.1.call-done = bf16[2,512,1536]{2,1,0:T(8,128)(2,1)} async-done(((bf16[2,32,1536]{2,1,0:T(8,128)(2,1)}), bf16[2,512,1536]{2,1,0:T(8,128)(2,1)}) %all-gather.8.cloned.1.call-update) | async-done | bytes 3145744 | tf_op jit(solution)/shard_map/all_gather | solution.py:199
  149.3 1.7 copy.61
  151.0 0.0 copy-start.6
  151.0 0.0 copy-start.7
  151.0 2.5 %convolution_convert_fusion = bf16[512,1536]{1,0:T(8,128)(2,1)} fusion(bf16[512,768]{0,1:T(8,128)(2,1)S(1)} %bitcast.58, bf16[768,1536]{1,0:T(8,128)(2,1)S(1)} %copy-done), kind=kOutput, calls=%fused_computation.12 | convolution fusion | flops 1208745984 | bytes 4718592 | tf_op jit(solution)/shard_map/dot_general | solution.py:232
  153.5 1.5 collective-permute-start.1
  155.0 0.1 fusion.24
  155.1 0.8 reduce-window.6
  155.9 0.2 slice_reduce_fusion
  156.1 0.2 reduce-window.9
  156.3 0.1 add_bitcast_fusion
  156.4 0.1 fusion.25
  156.5 0.2 select_reduce_fusion
  156.8 33.6 %collective-permute-done.1 = bf16[512,1536]{1,0:T(8,128)(2,1)} collective-permute-done((bf16[512,1536]{1,0:T(8,128)(2,1)}, bf16[512,1536]{1,0:T(8,128)(2,1)}, u32[]{:S(2)}, u32[]{:S(2)}) %collective-permute-start.1) | collective-permute-done | bytes 1572896 | tf_op jit(solution)/shard_map/ppermute | solution.py:135
  190.4 3.1 %multiply_reduce_fusion = (f32[512]{0:T(512)S(1)}, f32[512,1536]{1,0:T(8,128)S(1)}) fusion(bf16[512,1536]{1,0:T(8,128)(2,1)} %collective-permute-done.1, bf16[512,1536]{1,0:T(8,128)(2,1)} %convolution_convert_fusion, bf16[512,1536]{1,0:T(8,128)(2,1)} %copy-done.2), kind=kLoop, calls=%fused_computation.9 | loop fusion | flops 7077376 | bytes 7866368 | tf_op jit(solution)/shard_map/reduce_sum | solution.py:12
  193.6 0.9 convolution_convert_fusion.1
  194.5 2.1 copy-done.3
  196.6 0.8 fusion.34
  197.4 1.1 copy-done.9
  198.5 0.8 fusion.11
  199.3 4.6 %fusion.4 = bf16[512,1536]{1,0:T(8,128)(2,1)} fusion(bf16[2,192,512]{2,1,0:T(8,128)(2,1)S(1)} %fusion.11, bf16[2,512,1536]{2,1,0:T(8,128)(2,1)} %all-gather.8.cloned.1.call-done, f32[2,192]{1,0:T(2,128)S(1)} %select_reduce_fusion, s32[2,512]{1,0:T(2,128)S(1)} %bitcast.70, pred[2,512]{1,0:T(4,128)(4,1)S(1)} %broadcast_compare_fusion), kind=kOutput, calls=%fused_computation.11 | convolution fusion | flops 1210318848 | bytes 5118464 | tf_op jit(solution)/shard_map/ect,ecd->td/dot_general | solution.py:250
  203.9 1.2 constant_dynamic-slice_fusion
  205.1 1.5 collective-permute-start.2
  206.7 4.0 %copy.62 = bf16[1,4,2560,64]{2,3,1,0:T(8,128)(2,1)} copy(bf16[1,4,2560,64]{3,2,1,0:T(8,128)(2,1)} %bitcast.54) | data formatting | bytes 2621440
  210.6 4.0 %copy.63 = bf16[1,4,2560,64]{2,3,1,0:T(8,128)(2,1)} copy(bf16[1,4,2560,64]{3,2,1,0:T(8,128)(2,1)} %bitcast.52) | data formatting | bytes 2621440
  214.6 9.5 %collective-permute-done.2 = bf16[512,768]{1,0:T(8,128)(2,1)} collective-permute-done((bf16[512,768]{1,0:T(8,128)(2,1)S(1)}, bf16[512,768]{1,0:T(8,128)(2,1)}, u32[]{:S(2)}, u32[]{:S(2)}) %collective-permute-start.2) | collective-permute-done | bytes 786464 | tf_op jit(solution)/shard_map/ppermute | solution.py:135
  224.2 3.0 %fusion.13 = bf16[1,512,768]{2,1,0:T(8,128)(2,1)} fusion(bf16[512,768]{1,0:T(8,128)(2,1)} %collective-permute-done.2, f32[512,1536]{1,0:T(8,128)} %copy-done.1, s32[]{:T(128)S(6)} %select_n.68, bf16[512,1536]{1,0:T(8,128)(2,1)} %fusion.4), kind=kLoop, calls=%fused_computation.28 | loop fusion | flops 1966080 | bytes 3932164 | tf_op jit(solution)/shard_map/broadcast_in_dim | solution.py:256
  (27 shorter events, 0.1 us)
Async XLA Ops:
  7.2 143.8 %copy-start = (bf16[768,1536]{1,0:T(8,128)(2,1)S(1)}, bf16[768,1536]{1,0:T(8,128)(2,1)}, u32[]{:S(2)}) copy-start(bf16[768,1536]{1,0:T(8,128)(2,1)} %param.28) | copy-start | bytes 7077892
  7.2 136.6 %all-gather.4.cloned.1.call-start = ((), (), s32[]{:S(2)}) async-start(), calls=%async_computation | async-start | bytes 3342336 | tf_op jit(solution)/shard_map/all_gather | solution.py:197
  7.9 135.9 %all-gather.6.cloned.1.call-start = ((), (), s32[]{:S(2)}) async-start(), calls=%async_computation.1 | async-start | bytes 3342336 | tf_op jit(solution)/shard_map/all_gather | solution.py:198
  8.7 140.6 %all-gather.8.cloned.1.call-start = ((), (), s32[]{:S(2)}) async-start(), calls=%async_computation.2 | async-start | bytes 3342336 | tf_op jit(solution)/shard_map/all_gather | solution.py:199
  9.4 19.7 %collective-permute-start = (bf16[512,768]{1,0:T(8,128)(2,1)}, bf16[512,768]{1,0:T(8,128)(2,1)}, u32[]{:S(2)}, u32[]{:S(2)}) collective-permute-start(bf16[512,768]{1,0:T(8,128)(2,1)} %bitcast.62), channel_id=1, source_target_pairs={{0,1},{1,0},{2,3},{3,2},{4,5},{5,4},{6,7},{7,6},{8,9},{9,8},{10,11... | collective-permute-start | bytes 2359304 | tf_op jit(solution)/shard_map/ppermute | solution.py:135
  22.0 6.2 %copy-start.5 = (bf16[1,512,768]{2,1,0:T(8,128)(2,1)S(1)}, bf16[1,512,768]{2,1,0:T(8,128)(2,1)}, u32[]{:S(2)}) copy-start(bf16[1,512,768]{2,1,0:T(8,128)(2,1)} %param.16) | copy-start | bytes 2359300
  28.2 2.5 %copy-start.10 = (bf16[1536,256]{1,0:T(8,128)(2,1)S(1)}, bf16[1536,256]{1,0:T(8,128)(2,1)}, u32[]{:S(2)}) copy-start(bf16[1536,256]{1,0:T(8,128)(2,1)} %param.26) | copy-start | bytes 2359300
  28.2 2.5 %copy-start.11 = (f32[1536]{0:T(1024)S(1)}, f32[1536]{0:T(1024)}, u32[]{:S(2)}) copy-start(f32[1536]{0:T(1024)} %param.23) | copy-start | bytes 18436
  30.3 2.0 copy-start.2
  49.7 5.3 %copy-start.4 = (bf16[512,4,64]{2,0,1:T(8,128)(2,1)S(1)}, bf16[512,4,64]{2,0,1:T(8,128)(2,1)}, u32[]{:S(2)}) copy-start(bf16[512,4,64]{2,0,1:T(8,128)(2,1)} %copy.60) | copy-start | bytes 786436
  151.0 4.1 %copy-start.6 = (s32[1,512,8]{1,2,0:T(8,128)S(1)}, s32[1,512,8]{1,2,0:T(8,128)}, u32[]{:S(2)}) copy-start(s32[1,512,8]{1,2,0:T(8,128)} %param.21) | copy-start | bytes 49156
  151.0 5.4 %copy-start.7 = (f32[1,512,8]{1,2,0:T(8,128)S(1)}, f32[1,512,8]{1,2,0:T(8,128)}, u32[]{:S(2)}) copy-start(f32[1,512,8]{1,2,0:T(8,128)} %param.22) | copy-start | bytes 49156
  153.5 36.9 %collective-permute-start.1 = (bf16[512,1536]{1,0:T(8,128)(2,1)}, bf16[512,1536]{1,0:T(8,128)(2,1)}, u32[]{:S(2)}, u32[]{:S(2)}) collective-permute-start(bf16[512,1536]{1,0:T(8,128)(2,1)} %convolution_convert_fusion), channel_id=1, source_target_pairs={{0,1},{1,0},{2,3},{3,2},{4,5},{5,4},{6,7},{7,6},{8,9},{9,8},{10,11... | collective-permute-start | bytes 4718600 | tf_op jit(solution)/shard_map/ppermute | solution.py:135
  156.8 36.8 %copy-start.8 = (f32[1536]{0:T(1024)S(1)}, f32[1536]{0:T(1024)}, u32[]{:S(2)}) copy-start(f32[1536]{0:T(1024)} %param.24) | copy-start | bytes 18436
  193.5 3.8 %copy-start.1 = (f32[512,1536]{1,0:T(8,128)}, f32[512,1536]{1,0:T(8,128)S(1)}, u32[]{:S(2)}) copy-start(f32[512,1536]{1,0:T(8,128)S(1)} %get-tuple-element.24) | copy-start | bytes 9437188
  193.5 3.0 %copy-start.3 = (bf16[2,1536,512]{2,1,0:T(8,128)(2,1)S(1)}, bf16[2,1536,512]{2,1,0:T(8,128)(2,1)}, u32[]{:S(2)}) copy-start(bf16[2,1536,512]{2,1,0:T(8,128)(2,1)} %all-gather.4.cloned.1.call-done) | copy-start | bytes 9437188
  196.6 1.9 copy-start.9
  205.1 19.0 %collective-permute-start.2 = (bf16[512,768]{1,0:T(8,128)(2,1)S(1)}, bf16[512,768]{1,0:T(8,128)(2,1)}, u32[]{:S(2)}, u32[]{:S(2)}) collective-permute-start(bf16[512,768]{1,0:T(8,128)(2,1)S(1)} %constant_dynamic-slice_fusion), channel_id=1, source_target_pairs={{0,1},{1,0},{2,3},{3,2},{4,5},{5,4},{6,7},{7,6},{8,9},{9,8},{10,11... | collective-permute-start | bytes 2359304 | tf_op jit(solution)/shard_map/ppermute | solution.py:135
Sparse Core Ops, SparseCore 0:
  10.3 46.2 all-gather.3
  58.8 44.0 all-gather.5
  105.2 44.0 all-gather.7
